TPU v7x, 256 devices: a whole 4x4x8 slice. The times are simulated.
256 devices in a mesh: seq: 64 (over y, z, core), txt: 4 (over x).
Axes of the slice: x: 4, y: 4, z: 8, core: 2. Of those that a mesh axis runs over, the one named last changes fastest.
Arguments:
- self_q: bfloat16 [24576, 1024], P('seq', 'txt'), may hold values from -8 to 8
- self_k: bfloat16 [24576, 1024], P('seq', 'txt'), may hold values from -8 to 8
- self_v: bfloat16 [24576, 1024], P('seq', 'txt'), may hold values from -6 to 6
- cross_q: bfloat16 [24576, 1024], P('seq', 'txt'), may hold values from -8 to 8
- text_k: bfloat16 [4096, 1024], P('txt'), may hold values from -8 to 8
- text_v: bfloat16 [4096, 1024], P('txt'), may hold values from -6 to 6
- lags: int32 [192], P('seq'), may hold values from 1 to 32, as said below
Outputs:
- self_out: bfloat16 [24576, 1024], P('seq', 'txt')
- cross_out: bfloat16 [24576, 1024], P('seq', 'txt')
Inputs may be any that keep to these rules, and one draw needn't show every extreme that they name: lags never fall from one span to the next; the last span sees all 32 blocks.
All inputs are finite; a program needn't handle non-finite values.
Results may differ from a plain program's by a relative error of at most 0.014.
Values may be sent and summed in bfloat16 or wider, within the bound.
No kernel may reach another device: no remote copies, remote signals or barrier semaphores. Data moves between devices by JAX's collectives and lax.ppermute only.
A program may use at most 128 MiB of HBM per device.

v0:
```python
import math
import jax
import jax.numpy as jnp
from jax import lax
from jax.sharding import PartitionSpec as P

HSIZE = 128
SPAN = 128
TBLK = 128
NEG_FILL = -1e30


def scale_columns(weighted, scale):
    rows = weighted.shape[0]
    heads = scale.shape[0]
    shaped = weighted.reshape(rows, heads, weighted.shape[1] // heads)
    return (shaped * jnp.transpose(scale)[:, :, None]).reshape(rows, weighted.shape[1])


def softmax_update(state, query, keys, values, visible, factor):
    running, totals, weighted = state
    heads = running.shape[0]
    peaks = []
    sums = []
    columns = []
    for head in range(heads):
        low = head * HSIZE
        high = low + HSIZE
        scores = (
            lax.dot_general(
                query[:, low:high],
                keys[:, low:high],
                (((1,), (1,)), ((), ())),
                preferred_element_type=jnp.float32,
            )
            * factor
        )
        scores = jnp.where(visible, scores, NEG_FILL)
        peak = jnp.maximum(running[head], jnp.max(scores, axis=1))
        probs = jnp.where(visible, jnp.exp(scores - peak[:, None]), 0.0)
        shrink = jnp.exp(running[head] - peak)
        sums.append(totals[head] * shrink + jnp.sum(probs, axis=1))
        mixed = jnp.dot(
            probs.astype(jnp.bfloat16), values[:, low:high], preferred_element_type=jnp.float32
        )
        columns.append(weighted[:, low:high] * shrink[:, None] + mixed)
        peaks.append(peak)
    return (jnp.stack(peaks), jnp.stack(sums), jnp.concatenate(columns, axis=1))


def empty_state(heads, rows, width):
    return (
        jnp.full((heads, rows), NEG_FILL, jnp.float32),
        jnp.zeros((heads, rows), jnp.float32),
        jnp.zeros((rows, heads * width), jnp.float32),
    )


def finish(state):
    return scale_columns(state[2], 1.0 / state[1]).astype(jnp.bfloat16)


def per_device(self_q, self_k, self_v, cross_q, text_k, text_v, lags):
    rows = self_q.shape[0]
    half = rows // 2
    local_heads = self_q.shape[1] // HSIZE
    factor = 1.0 / math.sqrt(HSIZE)
    place = lax.axis_index("seq")
    offsets = jnp.arange(half, dtype=jnp.int32)
    lower = self_q[:half]
    upper = self_q[half:]
    upper_pos = place * rows + half + offsets
    positions = [place * rows + offsets, upper_pos]
    groups = [lower, upper]

    def visit(states, key_block, value_block, first, length):
        key_pos = first + jnp.arange(length, dtype=jnp.int32)
        updated = []
        for group in range(2):
            visible = key_pos[None, :] <= positions[group][:, None]
            query = groups[group]
            updated.append(
                lax.cond(
                    first <= positions[group][half - 1],
                    lambda state: softmax_update(
                        state, query, key_block, value_block, visible, factor
                    ),
                    lambda state: state,
                    states[group],
                )
            )
        return tuple(updated)

    initial = (empty_state(local_heads, half, HSIZE), empty_state(local_heads, half, HSIZE))
    carry = initial
    keys = lax.all_gather(self_k, "seq", axis=0, tiled=True)
    values = lax.all_gather(self_v, "seq", axis=0, tiled=True)
    length = keys.shape[0]
    block = 512
    width = keys.shape[1]
    key_blocks = keys.reshape(length // block, block, width)
    value_blocks = values.reshape(length // block, block, width)

    def one_block(states, inputs):
        key_block, value_block, number = inputs
        return (visit(states, key_block, value_block, number * block, block), None)

    carry, _ = lax.scan(
        one_block, carry, (key_blocks, value_blocks, jnp.arange(length // block, dtype=jnp.int32))
    )
    states = carry
    lower_out = finish(states[0])
    upper_out = finish(states[1])
    self_out = jnp.concatenate([lower_out, upper_out], axis=0)
    limits = jnp.repeat(lags * TBLK, SPAN)
    whole_keys, whole_values = (
        lax.all_to_all(text_k, "txt", split_axis=1, concat_axis=0, tiled=True),
        lax.all_to_all(text_v, "txt", split_axis=1, concat_axis=0, tiled=True),
    )
    text_rows = whole_keys.shape[0]
    visible = jnp.arange(text_rows, dtype=jnp.int32)[None, :] < limits[:, None]
    cross_state = softmax_update(
        empty_state(local_heads, rows, HSIZE), cross_q, whole_keys, whole_values, visible, factor
    )
    cross_out = finish(cross_state)
    return (self_out, cross_out)


def solution(mesh):
    return jax.shard_map(
        per_device,
        mesh=mesh,
        in_specs=(
            P("seq", "txt"),
            P("seq", "txt"),
            P("seq", "txt"),
            P("seq", "txt"),
            P("txt", None),
            P("txt", None),
            P("seq"),
        ),
        out_specs=(P("seq", "txt"), P("seq", "txt")),
        check_vma=False,
    )
```

profile of v0, /device:TPU:249, one launch (start us, length us, event | category | flops | bytes accessed | tf_op | source)
XLA Modules:
  0.0 571.9 jit_solution(3053998208419744763)
XLA Ops:
  8.6 3.9 copy.17
  12.6 4.1 all-to-all-start
  16.7 3.9 copy.19
  20.7 21.6 %all-to-all-done = bf16[1024,4,256]{0,2,1:T(8,128)(2,1)S(1)} async-done(((bf16[1024,4,256]{0,2,1:T(8,128)(2,1)}), bf16[1024,4,256]{0,2,1:T(8,128)(2,1)S(1)}, u32[]{:S(2)}, u32[]{:S(2)}) %all-to-all-start) | async-done | bytes 2097184 | tf_op jit(solution)/shard_map/all_to_all | solution.py:117
  42.2 4.6 all-to-all-start.1
  46.9 2.6 copy.18
  49.5 21.9 %all-to-all-done.1 = bf16[1024,4,256]{0,2,1:T(8,128)(2,1)} async-done(((bf16[1024,4,256]{0,2,1:T(8,128)(2,1)}), bf16[1024,4,256]{0,2,1:T(8,128)(2,1)}, u32[]{:S(2)}, u32[]{:S(2)}) %all-to-all-start.1) | async-done | bytes 2097184 | tf_op jit(solution)/shard_map/all_to_all | solution.py:118
  71.5 2.9 copy.20
  74.4 2.8 fusion.83
  78.6 3.3 fusion.48
  81.9 1.6 fusion.59
  83.6 1.6 fusion.56
  86.1 11.4 %all-gather.3.cloned.1.call-done = bf16[24576,256]{1,0:T(8,128)(2,1)} async-done(((bf16[384,256]{1,0:T(8,128)(2,1)}), bf16[24576,256]{1,0:T(8,128)(2,1)}) %all-gather.3.cloned.1.call-update) | async-done | bytes 12582928 | tf_op jit(solution)/shard_map/all_gather | solution.py:96
  97.5 89.2 %all-gather.5.cloned.1.call-done = bf16[24576,256]{1,0:T(8,128)(2,1)} async-done(((bf16[384,256]{1,0:T(8,128)(2,1)}), bf16[24576,256]{1,0:T(8,128)(2,1)}) %all-gather.5.cloned.1.call-update) | async-done | bytes 12582928 | tf_op jit(solution)/shard_map/all_gather | solution.py:97
  186.7 376.7 %while.20 = (s32[]{:T(128)}, f32[2,192]{1,0:T(2,128)S(1)}, f32[2,192]{1,0:T(2,128)S(1)}, f32[192,256]{1,0:T(8,128)S(1)}, f32[2,192]{1,0:T(2,128)S(1)}, /*index=5...) while((s32[]{:T(128)}, f32[2,192]{1,0:T(2,128)S(1)}, ...), condition=%wide.region_13.14_spmd, body=%wide.region_0.13_spmd.sunk | while | flops 206148608 | bytes 8684505 | solution.py:108
  190.2 1.6 conditional.4
  198.0 1.6 conditional.4
  205.9 1.6 conditional.4
  213.7 1.6 conditional.4
  221.6 1.6 conditional.4
  229.4 1.6 conditional.4
  237.3 1.6 conditional.4
  245.1 1.6 conditional.4
  253.0 1.6 conditional.4
  284.4 1.6 conditional.4
  292.2 1.6 conditional.4
  300.1 1.6 conditional.4
  307.9 1.6 conditional.4
  315.8 1.6 conditional.4
  323.6 1.6 conditional.4
  331.5 1.6 conditional.4
  339.3 1.6 conditional.4
  (1416 shorter events, 417.6 us)
Async XLA Ops:
  7.2 90.3 %all-gather.3.cloned.1.call-start = ((), (), s32[]{:S(2)}) async-start(), calls=%async_computation.2 | async-start | bytes 12779520 | tf_op jit(solution)/shard_map/all_gather | solution.py:96
  7.9 178.8 %all-gather.5.cloned.1.call-start = ((), (), s32[]{:S(2)}) async-start(), calls=%async_computation.3 | async-start | bytes 12779520 | tf_op jit(solution)/shard_map/all_gather | solution.py:97
  12.6 34.2 %copy-start.3 = (s32[3]{0:T(128)S(1)}, s32[3]{0:T(128)}, u32[]{:S(2)}) copy-start(s32[3]{0:T(128)} %param.19) | copy-start | bytes 40
  12.6 34.3 %copy-start.1 = (bf16[384,256]{1,0:T(8,128)(2,1)S(1)}, bf16[384,256]{1,0:T(8,128)(2,1)}, u32[]{:S(2)}) copy-start(bf16[384,256]{1,0:T(8,128)(2,1)} %param.13) | copy-start | bytes 589828
  12.6 29.6 %all-to-all-start = ((bf16[1024,4,256]{0,2,1:T(8,128)(2,1)}), bf16[1024,4,256]{0,2,1:T(8,128)(2,1)S(1)}, u32[]{:S(2)}, u32[]{:S(2)}) async-start(bf16[1024,4,256]{0,2,1:T(8,128)(2,1)} %bitcast.57), calls=%async_computation | async-start | bytes 4194304 | tf_op jit(solution)/shard_map/all_to_all | solution.py:117
  42.2 32.2 %copy-start.2 = (bf16[384,256]{1,0:T(8,128)(2,1)S(1)}, bf16[384,256]{1,0:T(8,128)(2,1)}, u32[]{:S(2)}) copy-start(bf16[384,256]{1,0:T(8,128)(2,1)} %param.16) | copy-start | bytes 589828
  42.2 29.3 %all-to-all-start.1 = ((bf16[1024,4,256]{0,2,1:T(8,128)(2,1)}), bf16[1024,4,256]{0,2,1:T(8,128)(2,1)}, u32[]{:S(2)}, u32[]{:S(2)}) async-start(bf16[1024,4,256]{0,2,1:T(8,128)(2,1)} %bitcast.56), calls=%async_computation.1 | async-start | bytes 4194304 | tf_op jit(solution)/shard_map/all_to_all | solution.py:118
  74.4 2.8 copy-start
Sparse Core Ops, SparseCore 0:
  10.7 86.6 all-gather.2
  100.2 86.4 all-gather.4
where the time goes:
time: 574 us; the launch traced here: 572 us
  local copies, waits for them, and re-layouts  149 us (26%)
  waiting for transfers between devices  145 us (25%)
  matrix products  118 us (21%)
  loops' own time  93.5 us (16%)
  other arithmetic  42.7 us (7%)
  between operations  14.3 us (2%)
  starting transfers between devices  8.81 us (2%)
    all_gather x1, waiting for transfers between devices, per_device(): values = lax.all_gather(self_v, 'seq', axis=0, tiled=True)  89.2 us
    another operation x1, loops' own time, per_device(): lax.scan(one_block, carry, (key_blocks, value_blocks, jnp.arange(length /...  86.1 us
    dot_general x194, matrix products, softmax_update(): lax.dot_general(query[:, low:high], keys[:, low:high], (((1,), (1,)), (()...  63.3 us
    dot_general x194, matrix products, softmax_update(): jnp.dot(probs.astype(jnp.bfloat16), values[:, low:high], preferred_elemen...  54.7 us
    slice x96, local copies, waits for them, and re-layouts, visit(): positions[group][half - 1]  53 us
    squeeze x48, local copies, waits for them, and re-layouts, per_device(): lax.scan(one_block, carry, (key_blocks, value_blocks, jnp.arange(length /...  51.4 us
    reduce_sum x97, other arithmetic, softmax_update(): sums.append(totals[head] * shrink + jnp.sum(probs, axis=1))  36 us
    dynamic_slice x48, local copies, waits for them, and re-layouts, per_device(): lax.scan(one_block, carry, (key_blocks, value_blocks, jnp.arange(length /...  29.3 us
  transfers between devices with their start and end apart: 4, of which 4 were waited for; matrix products, arithmetic and copies ran while one was open for 4% of the time, Pallas kernels for 0%

commit v1 on v0

--- a/solution.py
+++ b/solution.py
@@ -94,7 +94,9 @@
     initial = (empty_state(local_heads, half, HSIZE), empty_state(local_heads, half, HSIZE))
     carry = initial
     keys = lax.all_gather(self_k, "seq", axis=0, tiled=True)
-    values = lax.all_gather(self_v, "seq", axis=0, tiled=True)
+    values = jnp.concatenate(
+        lax.all_to_all(jnp.stack([self_v] * lax.axis_size("seq")), "seq", 0, 0), axis=0
+    )
     length = keys.shape[0]
     block = 512
     width = keys.shape[1]

time: 574 us -> 799 us (1.39)
  waiting for transfers between devices: 145 us -> 303 us
  blocking collectives: 0 us -> 28.2 us
  local copies, waits for them, and re-layouts: 149 us -> 167 us
    all_to_all x1, waiting for transfers between devices: 21.9 us -> 281 us  [per_device(): lax.all_to_all(jnp.stack([self_v] * lax.axis_size('seq')), 'seq', 0, 0)]
    all_gather x1 -> x0, waiting for transfers between devices: 89.2 us -> none  [per_device(): values = lax.all_gather(self_v, 'seq', axis=0, tiled=True)]
    all_to_all x0 -> x1, blocking collectives: none -> 28.2 us  [per_device(): lax.all_to_all(text_v, 'txt', split_axis=1, concat_axis=0, tiled=True)]
    all_gather x1, waiting for transfers between devices: 11.4 us -> 0.01 us  [per_device(): keys = lax.all_gather(self_k, 'seq', axis=0, tiled=True)]
    slice x96, local copies, waits for them, and re-layouts: 53 us -> 61.1 us  [visit(): positions[group][half - 1]]
  transfers between devices with their start and end apart: 4 -> 3, of which waited for: 4 -> 2; matrix products, arithmetic and copies ran while one was open for 4% -> 4% of each run, Pallas kernels for 0% -> 0%
where the time goes in v1:
time: 799 us; the launch traced here: 796 us
  waiting for transfers between devices  303 us (38%)
  local copies, waits for them, and re-layouts  167 us (21%)
  matrix products  125 us (16%)
  loops' own time  99.7 us (12%)
  other arithmetic  42.2 us (5%)
  blocking collectives  28.2 us (4%)
  starting transfers between devices  15.9 us (2%)
  between operations  14.3 us (2%)
    all_to_all x1, waiting for transfers between devices, per_device(): lax.all_to_all(jnp.stack([self_v] * lax.axis_size('seq')), 'seq', 0, 0)  281 us
    another operation x1, loops' own time, per_device(): lax.scan(one_block, carry, (key_blocks, value_blocks, jnp.arange(length /...  92.6 us
    dot_general x194, matrix products, softmax_update(): lax.dot_general(query[:, low:high], keys[:, low:high], (((1,), (1,)), (()...  63.9 us
    slice x96, local copies, waits for them, and re-layouts, visit(): positions[group][half - 1]  61.1 us
    dot_general x194, matrix products, softmax_update(): jnp.dot(probs.astype(jnp.bfloat16), values[:, low:high], preferred_elemen...  60.9 us
    squeeze x48, local copies, waits for them, and re-layouts, per_device(): lax.scan(one_block, carry, (key_blocks, value_blocks, jnp.arange(length /...  51.4 us
    reduce_sum x97, other arithmetic, softmax_update(): sums.append(totals[head] * shrink + jnp.sum(probs, axis=1))  35.5 us
    dynamic_slice x48, local copies, waits for them, and re-layouts, per_device(): lax.scan(one_block, carry, (key_blocks, value_blocks, jnp.arange(length /...  30.9 us
  transfers between devices with their start and end apart: 3, of which 2 were waited for; matrix products, arithmetic and copies ran while one was open for 4% of the time, Pallas kernels for 0%

profile of v1, /device:TPU:249, one launch (start us, length us, event | category | flops | bytes accessed | tf_op | source)
XLA Modules:
  0.0 795.7 jit_solution(5258924134853230812)
XLA Ops:
  7.2 3.9 copy.17
  11.1 4.1 all-to-all-start.1
  15.3 3.9 copy.19
  19.2 21.5 %all-to-all-done.1 = bf16[1024,4,256]{0,2,1:T(8,128)(2,1)S(1)} async-done(((bf16[1024,4,256]{0,2,1:T(8,128)(2,1)}), bf16[1024,4,256]{0,2,1:T(8,128)(2,1)S(1)}, u32[]{:S(2)}, u32[]{:S(2)}) %all-to-all-start.1) | async-done | bytes 2097184 | tf_op jit(solution)/shard_map/all_to_all | solution.py:119
  42.0 28.2 %all_to_all.43 = bf16[1024,4,256]{0,2,1:T(8,128)(2,1)S(1)} all-to-all(bf16[1024,4,256]{0,2,1:T(8,128)(2,1)} %bitcast.58), channel_id=1, replica_groups=mesh['seq'=64,'txt'=4] {'txt'}, dimensions={1} | all-to-all | bytes 4194304 | tf_op jit(solution)/shard_map/all_to_all | solution.py:120
  70.2 6.1 stack.12
  76.3 11.6 %all-to-all-start = ((bf16[64,384,256]{2,1,0:T(8,128)(2,1)}), bf16[64,384,256]{2,1,0:T(8,128)(2,1)}, u32[]{:S(2)}, u32[]{:S(2)}) async-start(bf16[64,384,256]{2,1,0:T(8,128)(2,1)} %stack.12), calls=%async_computation | async-start | bytes 25165824 | tf_op jit(solution)/shard_map/all_to_all | solution.py:98
  88.8 3.9 copy.18
  92.7 2.7 fusion.83
  96.8 3.3 fusion.48
  100.2 2.6 copy.20
  102.8 5.0 fusion.56
  107.8 4.5 fusion.59
  113.1 281.2 %all-to-all-done = bf16[64,384,256]{2,1,0:T(8,128)(2,1)} async-done(((bf16[64,384,256]{2,1,0:T(8,128)(2,1)}), bf16[64,384,256]{2,1,0:T(8,128)(2,1)}, u32[]{:S(2)}, u32[]{:S(2)}) %all-to-all-start) | async-done | bytes 12582944 | tf_op jit(solution)/shard_map/all_to_all | solution.py:98
  394.4 392.9 %while.20 = (s32[]{:T(128)}, f32[2,192]{1,0:T(2,128)S(1)}, f32[2,192]{1,0:T(2,128)S(1)}, f32[192,256]{1,0:T(8,128)S(1)}, f32[2,192]{1,0:T(2,128)S(1)}, /*index=5...) while((s32[]{:T(128)}, f32[2,192]{1,0:T(2,128)S(1)}, ...), condition=%wide.region_13.14_spmd, body=%wide.region_0.13_spmd.sunk | while | flops 206148608 | bytes 8684497 | solution.py:110
  433.7 1.6 conditional.4
  441.9 1.6 conditional.4
  450.1 1.6 conditional.4
  482.8 1.6 conditional.4
  491.0 1.6 conditional.4
  499.2 1.6 conditional.4
  531.9 1.6 conditional.4
  540.1 1.6 conditional.4
  548.3 1.6 conditional.4
  556.5 1.6 conditional.4
  589.2 1.6 conditional.4
  597.4 1.6 conditional.4
  605.6 1.6 conditional.4
  638.3 1.6 conditional.4
  646.5 1.6 conditional.4
  654.7 1.6 conditional.4
  687.4 1.6 conditional.4
  (1425 shorter events, 428.1 us)
Async XLA Ops:
  11.1 59.1 %copy-start.6 = (bf16[384,256]{1,0:T(8,128)(2,1)S(1)}, bf16[384,256]{1,0:T(8,128)(2,1)}, u32[]{:S(2)}) copy-start(bf16[384,256]{1,0:T(8,128)(2,1)} %param.15) | copy-start | bytes 589828
  11.1 29.6 %all-to-all-start.1 = ((bf16[1024,4,256]{0,2,1:T(8,128)(2,1)}), bf16[1024,4,256]{0,2,1:T(8,128)(2,1)S(1)}, u32[]{:S(2)}, u32[]{:S(2)}) async-start(bf16[1024,4,256]{0,2,1:T(8,128)(2,1)} %bitcast.57), calls=%async_computation.1 | async-start | bytes 4194304 | tf_op jit(solution)/shard_map/all_to_all | solution.py:119
  40.7 1.3 copy-start
  76.3 12.3 %copy-start.8 = (s32[3]{0:T(128)S(1)}, s32[3]{0:T(128)}, u32[]{:S(2)}) copy-start(s32[3]{0:T(128)} %param.19) | copy-start | bytes 40
  76.3 12.4 %copy-start.5 = (bf16[384,256]{1,0:T(8,128)(2,1)S(1)}, bf16[384,256]{1,0:T(8,128)(2,1)}, u32[]{:S(2)}) copy-start(bf16[384,256]{1,0:T(8,128)(2,1)} %param.13) | copy-start | bytes 589828
  76.3 16.4 %copy-start.7 = (bf16[384,256]{1,0:T(8,128)(2,1)S(1)}, bf16[384,256]{1,0:T(8,128)(2,1)}, u32[]{:S(2)}) copy-start(bf16[384,256]{1,0:T(8,128)(2,1)} %param.16) | copy-start | bytes 589828
  76.3 318.0 %all-to-all-start = ((bf16[64,384,256]{2,1,0:T(8,128)(2,1)}), bf16[64,384,256]{2,1,0:T(8,128)(2,1)}, u32[]{:S(2)}, u32[]{:S(2)}) async-start(bf16[64,384,256]{2,1,0:T(8,128)(2,1)} %stack.12), calls=%async_computation | async-start | bytes 25165824 | tf_op jit(solution)/shard_map/all_to_all | solution.py:98
  87.9 306.4 %all-gather.2.cloned.1.call-start = ((), (), s32[]{:S(2)}) async-start(), calls=%async_computation.3 | async-start | bytes 12779520 | tf_op jit(solution)/shard_map/all_gather | solution.py:96
  92.7 2.7 copy-start.4
  95.4 4.7 copy-start.1
  96.8 3.3 copy-start.2
  102.8 5.0 copy-start.3
Sparse Core Ops, SparseCore 0:
  91.5 172.7 all-gather.1
